TPU v7x, 128 devices: a whole 4x4x4 slice. The times are simulated.
128 devices in a mesh: kv: 16 (over y, x), seq: 8 (over z, core).
Axes of the slice: x: 4, y: 4, z: 4, core: 2. Of those that a mesh axis runs over, the one named last changes fastest.
Arguments:
- prefill_keys: bfloat16 [262144, 1024], P(('kv', 'seq')), may hold values from -50 to 50
- queries: bfloat16 [1024, 8192], P('seq'), may hold values from -6 to 6
- outlier_spans: int32 [512], P(('kv', 'seq')), may hold values from 0 to 255
- start_basis: float32 [160, 1024], replicated, may hold values from -6 to 6
Outputs:
- basis: float32 [160, 1024], replicated
- coefficients: bfloat16 [160, 262144], P(None, ('kv', 'seq'))
- landmark_scores: bfloat16 [8, 1024, 32768], P(None, 'seq', 'kv')
- outlier_scores: bfloat16 [8, 1024, 4096], P(None, 'seq', 'kv')
Inputs may be any that keep to these rules, and one draw needn't show every extreme that they name: `outlier_spans`: entries index spans of 8 rows among the rows held by the same device.
All inputs are finite; a program needn't handle non-finite values.
Results may differ from a plain program's by a relative error of at most 0.0037.
Values may be sent and summed in bfloat16 or wider, within the bound.
No kernel may reach another device: no remote copies, remote signals or barrier semaphores. Data moves between devices by JAX's collectives and lax.ppermute only.
A program may use at most 128 MiB of HBM per device.

v0:
```python
import math
import jax
import jax.numpy as jnp
from jax import lax
from jax.sharding import PartitionSpec as P

KVH = 8
HEAD = 128
GROUP = 8
ITERS = 8
SPAN = 8


def moment_of(product):
    return jnp.dot(
        product, product.T, precision=lax.Precision.HIGHEST, preferred_element_type=jnp.float32
    )


def solve_lower(moment, product):
    return jax.scipy.linalg.solve_triangular(jnp.linalg.cholesky(moment), product, lower=True)


def apply_gram(subspace, gram_rows):
    return lax.dot_general(
        subspace,
        gram_rows,
        (((1,), (1,)), ((), ())),
        precision=lax.Precision.HIGHEST,
        preferred_element_type=jnp.float32,
    )


def local(prefill_keys, queries, outlier_spans, start_basis):
    rows_dev = prefill_keys.shape[0]
    width = prefill_keys.shape[1]
    inverse_tokens = 1.0 / (rows_dev * lax.axis_size("kv") * lax.axis_size("seq"))
    scale_factor = 1.0 / math.sqrt(HEAD)
    spanned = prefill_keys.reshape(rows_dev // SPAN, SPAN, width)
    landmarks = jnp.mean(spanned, axis=1, dtype=jnp.float32).astype(jnp.bfloat16)
    picked = jnp.take(spanned, outlier_spans, axis=0).reshape(-1, width)
    query_count = queries.shape[0]
    query_heads = jnp.transpose(queries.reshape(query_count, KVH, GROUP, HEAD), (1, 0, 2, 3))

    def score_rows(shard_rows):
        count_rows = shard_rows.shape[0]
        key_heads = jnp.swapaxes(shard_rows.reshape(count_rows, KVH, HEAD), 0, 1)

        def one_head(pairing):
            query_group, key_group = pairing
            scores = jnp.einsum(
                "qgd,cd->qgc", query_group, key_group, preferred_element_type=jnp.float32
            )
            return jnp.max(scores, axis=1)

        return (lax.map(one_head, (query_heads, key_heads)) * scale_factor).astype(jnp.bfloat16)

    landmark_scores = score_rows(lax.all_gather(landmarks, "seq", axis=0, tiled=True))
    outlier_scores = score_rows(lax.all_gather(picked, "seq", axis=0, tiled=True))
    subspace = start_basis
    gram_block = lax.psum_scatter(
        lax.dot_general(
            prefill_keys, prefill_keys, (((0,), (0,)), ((), ())), preferred_element_type=jnp.float32
        )
        * inverse_tokens,
        "kv",
        scatter_dimension=0,
        tiled=True,
    )
    gram_rows = lax.psum(gram_block, "seq")
    for iteration in range(ITERS):
        product = apply_gram(subspace, gram_rows)
        moment = lax.psum(moment_of(product), "kv")
        basis_piece = solve_lower(moment, product)
        subspace = lax.all_gather(basis_piece, "kv", axis=1, tiled=True)
    rounded = subspace.astype(jnp.bfloat16)
    coefficients = lax.dot_general(
        rounded, prefill_keys, (((1,), (1,)), ((), ())), preferred_element_type=jnp.float32
    ).astype(jnp.bfloat16)
    return (subspace, coefficients, landmark_scores, outlier_scores)


def solution(mesh):
    placed = (P(("kv", "seq"), None), P("seq", None), P(("kv", "seq")), P())
    return jax.shard_map(
        local,
        mesh=mesh,
        in_specs=placed,
        out_specs=(P(), P(None, ("kv", "seq")), P(None, "seq", "kv"), P(None, "seq", "kv")),
        check_vma=False,
    )
```

profile of v0, /device:TPU:0, one launch (start us, length us, event | category | flops | bytes accessed | tf_op | source)
XLA Modules:
  0.0 1433.7 jit_solution(11385063445946750643)
XLA Ops:
  7.2 10.1 convolution_multiply_fusion
  17.4 80.1 %reduce-scatter.2.cloned.1.call-done = f32[64,1024]{1,0:T(8,128)} async-done(((f32[1024,1024]{1,0:T(8,128)}), f32[64,1024]{1,0:T(8,128)}) %reduce-scatter.2.cloned.1.call-update) | async-done | bytes 262160 | tf_op jit(solution)/shard_map/reduce_scatter | solution.py:61
  97.5 61.8 %all-reduce.13.cloned.1.call-done = f32[64,1024]{1,0:T(8,128)} async-done(((f32[64,1024]{1,0:T(8,128)}), f32[64,1024]{1,0:T(8,128)}) %all-reduce.13.cloned.1.call-update) | async-done | bytes 262160 | tf_op jit(solution)/shard_map/psum | solution.py:70
  162.7 82.6 %all-reduce.15.cloned.1.call-done = f32[160,160]{0,1:T(8,128)} async-done(((f32[160,160]{0,1:T(8,128)}), f32[160,160]{0,1:T(8,128)}) %all-reduce.15.cloned.1.call-update) | async-done | bytes 102416 | tf_op jit(solution)/shard_map/psum | solution.py:73
  247.3 11.7 cholesky.412
  259.1 9.8 custom-call.25
  274.9 19.7 %custom-call.26 = f32[2,128,128]{1,2,0:T(8,128)S(1)} custom-call(f32[2,128,128]{2,1,0:T(8,128)S(1)} %pad_maximum_fusion), custom_call_target="InvertDiagBlocksLowerTriangular" | custom-call | tf_op jit(solution)/shard_map/jit(_solve_triangular)/triangular_solve | solution.py:21
  295.1 23.2 %all_gather.30 = f32[160,1024]{0,1:T(8,128)S(1)} all-gather(f32[160,64]{0,1:T(8,128)S(1)} %pad_maximum_fusion.8), channel_id=1, replica_groups=mesh['kv'=16,'seq'=8] {'kv'}, dimensions={1}, use_global_device_ids=true | all-gather | bytes 696320 | tf_op jit(solution)/shard_map/all_gather | solution.py:75
  320.3 82.5 %all-reduce.17.cloned.1.call-done = f32[160,160]{0,1:T(8,128)} async-done(((f32[160,160]{0,1:T(8,128)}), f32[160,160]{0,1:T(8,128)}) %all-reduce.17.cloned.1.call-update) | async-done | bytes 102416 | tf_op jit(solution)/shard_map/psum | solution.py:73
  404.8 11.7 cholesky.450
  416.5 9.8 custom-call.27
  432.4 19.7 %custom-call.28 = f32[2,128,128]{1,2,0:T(8,128)S(1)} custom-call(f32[2,128,128]{2,1,0:T(8,128)S(1)} %pad_maximum_fusion.1), custom_call_target="InvertDiagBlocksLowerTriangular" | custom-call | tf_op jit(solution)/shard_map/jit(_solve_triangular)/triangular_solve | solution.py:21
  452.6 23.2 %all_gather.31 = f32[160,1024]{0,1:T(8,128)S(1)} all-gather(f32[160,64]{0,1:T(8,128)S(1)} %pad_maximum_fusion.9), channel_id=1, replica_groups=mesh['kv'=16,'seq'=8] {'kv'}, dimensions={1}, use_global_device_ids=true | all-gather | bytes 696320 | tf_op jit(solution)/shard_map/all_gather | solution.py:75
  478.0 82.3 %all-reduce.19.cloned.1.call-done = f32[160,160]{0,1:T(8,128)} async-done(((f32[160,160]{0,1:T(8,128)}), f32[160,160]{0,1:T(8,128)}) %all-reduce.19.cloned.1.call-update) | async-done | bytes 102416 | tf_op jit(solution)/shard_map/psum | solution.py:73
  562.2 11.7 cholesky.488
  574.0 9.8 custom-call.29
  589.8 19.7 %custom-call.30 = f32[2,128,128]{1,2,0:T(8,128)S(1)} custom-call(f32[2,128,128]{2,1,0:T(8,128)S(1)} %pad_maximum_fusion.2), custom_call_target="InvertDiagBlocksLowerTriangular" | custom-call | tf_op jit(solution)/shard_map/jit(_solve_triangular)/triangular_solve | solution.py:21
  610.1 23.2 %all_gather.32 = f32[160,1024]{0,1:T(8,128)S(1)} all-gather(f32[160,64]{0,1:T(8,128)S(1)} %pad_maximum_fusion.10), channel_id=1, replica_groups=mesh['kv'=16,'seq'=8] {'kv'}, dimensions={1}, use_global_device_ids=true | all-gather | bytes 696320 | tf_op jit(solution)/shard_map/all_gather | solution.py:75
  640.7 77.0 %all-reduce.21.cloned.1.call-done = f32[160,160]{0,1:T(8,128)} async-done(((f32[160,160]{0,1:T(8,128)}), f32[160,160]{0,1:T(8,128)}) %all-reduce.21.cloned.1.call-update) | async-done | bytes 102416 | tf_op jit(solution)/shard_map/psum | solution.py:73
  719.7 11.7 cholesky.526
  731.5 9.8 custom-call.31
  747.3 19.7 %custom-call.32 = f32[2,128,128]{1,2,0:T(8,128)S(1)} custom-call(f32[2,128,128]{2,1,0:T(8,128)S(1)} %pad_maximum_fusion.3), custom_call_target="InvertDiagBlocksLowerTriangular" | custom-call | tf_op jit(solution)/shard_map/jit(_solve_triangular)/triangular_solve | solution.py:21
  767.5 23.2 %all_gather.33 = f32[160,1024]{0,1:T(8,128)S(1)} all-gather(f32[160,64]{0,1:T(8,128)S(1)} %pad_maximum_fusion.11), channel_id=1, replica_groups=mesh['kv'=16,'seq'=8] {'kv'}, dimensions={1}, use_global_device_ids=true | all-gather | bytes 696320 | tf_op jit(solution)/shard_map/all_gather | solution.py:75
  802.4 13.6 all_gather.39
  816.2 15.8 %while.30 = (s32[]{:T(128)}, f32[8,128,256]{2,1,0:T(8,128)}, bf16[8,128,8,128]{3,1,2,0:T(8,128)(2,1)}, bf16[8,256,128]{1,2,0:T(8,128)(2,1)S(1)}, s32[]{:T(128)}) while((s32[]{:T(128)}, f32[8,128,256]{2,1,0:T(8,128)}, bf16[8,128,8,128]{3,1,2,0:T(8,128)(2,1)}, bf16[8,256,128]{1,2,0:T(8,128)(2,1)S(1)}, s32[]{:T(128)}) %tuple.133), condition=%wide.region_20.23_spmd, body=%wide.region_18.22_spmd.sunk | while | flops 67338240 | bytes 722493 | solution.py:56
  832.0 43.2 %all-reduce.23.cloned.1.call-done = f32[160,160]{0,1:T(8,128)} async-done(((f32[160,160]{0,1:T(8,128)}), f32[160,160]{0,1:T(8,128)}) %all-reduce.23.cloned.1.call-update) | async-done | bytes 102416 | tf_op jit(solution)/shard_map/psum | solution.py:73
  877.2 11.7 cholesky.564
  888.9 9.8 custom-call.33
  904.8 19.7 %custom-call.34 = f32[2,128,128]{1,2,0:T(8,128)S(1)} custom-call(f32[2,128,128]{2,1,0:T(8,128)S(1)} %pad_maximum_fusion.4), custom_call_target="InvertDiagBlocksLowerTriangular" | custom-call | tf_op jit(solution)/shard_map/jit(_solve_triangular)/triangular_solve | solution.py:21
  925.0 23.2 %all_gather.34 = f32[160,1024]{0,1:T(8,128)S(1)} all-gather(f32[160,64]{0,1:T(8,128)S(1)} %pad_maximum_fusion.12), channel_id=1, replica_groups=mesh['kv'=16,'seq'=8] {'kv'}, dimensions={1}, use_global_device_ids=true | all-gather | bytes 696320 | tf_op jit(solution)/shard_map/all_gather | solution.py:75
  950.9 6.6 copy.121
  957.5 75.2 %all-reduce.25.cloned.1.call-done = f32[160,160]{0,1:T(8,128)} async-done(((f32[160,160]{0,1:T(8,128)}), f32[160,160]{0,1:T(8,128)}) %all-reduce.25.cloned.1.call-update) | async-done | bytes 102416 | tf_op jit(solution)/shard_map/psum | solution.py:73
  1034.6 11.7 cholesky.602
  1046.4 9.8 custom-call.35
  1062.2 19.7 %custom-call.36 = f32[2,128,128]{1,2,0:T(8,128)S(1)} custom-call(f32[2,128,128]{2,1,0:T(8,128)S(1)} %pad_maximum_fusion.5), custom_call_target="InvertDiagBlocksLowerTriangular" | custom-call | tf_op jit(solution)/shard_map/jit(_solve_triangular)/triangular_solve | solution.py:21
  1082.5 23.2 %all_gather.35 = f32[160,1024]{0,1:T(8,128)S(1)} all-gather(f32[160,64]{0,1:T(8,128)S(1)} %pad_maximum_fusion.13), channel_id=1, replica_groups=mesh['kv'=16,'seq'=8] {'kv'}, dimensions={1}, use_global_device_ids=true | all-gather | bytes 696320 | tf_op jit(solution)/shard_map/all_gather | solution.py:75
  1107.5 28.5 %while.29 = (s32[]{:T(128)}, f32[8,128,2048]{2,1,0:T(8,128)}, bf16[8,128,8,128]{3,1,2,0:T(8,128)(2,1)}, bf16[8,2048,128]{1,2,0:T(8,128)(2,1)}, s32[]{:T(128)}) while((s32[]{:T(128)}, f32[8,128,2048]{2,1,0:T(8,128)}, bf16[8,128,8,128]{3,1,2,0:T(8,128)(2,1)}, bf16[8,2048,128]{1,2,0:T(8,128)(2,1)}, s32[]{:T(128)}) %tuple.132), condition=%wide.region_17.20_spmd, body=%wide.region_15.19_spmd.sunk | while | flops 538705920 | bytes 3933757 | solution.py:56
  1136.0 54.1 %all-reduce.27.cloned.1.call-done = f32[160,160]{0,1:T(8,128)} async-done(((f32[160,160]{0,1:T(8,128)}), f32[160,160]{0,1:T(8,128)}) %all-reduce.27.cloned.1.call-update) | async-done | bytes 102416 | tf_op jit(solution)/shard_map/psum | solution.py:73
  1192.1 11.7 cholesky.640
  1203.9 9.8 custom-call.37
  1219.7 19.7 %custom-call.38 = f32[2,128,128]{1,2,0:T(8,128)S(1)} custom-call(f32[2,128,128]{2,1,0:T(8,128)S(1)} %pad_maximum_fusion.6), custom_call_target="InvertDiagBlocksLowerTriangular" | custom-call | tf_op jit(solution)/shard_map/jit(_solve_triangular)/triangular_solve | solution.py:21
  1239.9 23.4 %all_gather.36 = f32[160,1024]{0,1:T(8,128)S(1)} all-gather(f32[160,64]{0,1:T(8,128)S(1)} %pad_maximum_fusion.14), channel_id=1, replica_groups=mesh['kv'=16,'seq'=8] {'kv'}, dimensions={1}, use_global_device_ids=true | all-gather | bytes 696320 | tf_op jit(solution)/shard_map/all_gather | solution.py:75
  1265.1 6.6 multiply_convert_fusion
  1271.7 76.1 %all-reduce.29.cloned.1.call-done = f32[160,160]{0,1:T(8,128)} async-done(((f32[160,160]{0,1:T(8,128)}), f32[160,160]{0,1:T(8,128)}) %all-reduce.29.cloned.1.call-update) | async-done | bytes 102416 | tf_op jit(solution)/shard_map/psum | solution.py:73
  1349.8 11.7 cholesky.678
  1361.6 9.8 custom-call.39
  1377.4 19.7 %custom-call.40 = f32[2,128,128]{1,2,0:T(8,128)S(1)} custom-call(f32[2,128,128]{2,1,0:T(8,128)S(1)} %pad_maximum_fusion.7), custom_call_target="InvertDiagBlocksLowerTriangular" | custom-call | tf_op jit(solution)/shard_map/jit(_solve_triangular)/triangular_solve | solution.py:21
  1397.7 23.3 %all_gather.37 = f32[160,1024]{0,1:T(8,128)S(1)} all-gather(f32[160,64]{0,1:T(8,128)S(1)} %pad_maximum_fusion.15), channel_id=1, replica_groups=mesh['kv'=16,'seq'=8] {'kv'}, dimensions={1}, use_global_device_ids=true | all-gather | bytes 696320 | tf_op jit(solution)/shard_map/all_gather | solution.py:75
  (259 shorter events, 140.0 us)
Async XLA Ops:
  7.2 152.2 %copy-start = (f32[160,1024]{1,0:T(8,128)S(1)}, f32[160,1024]{1,0:T(8,128)}, u32[]{:S(2)}) copy-start(f32[160,1024]{1,0:T(8,128)} %param.14) | copy-start | bytes 1966084
  7.2 90.3 %reduce-scatter.2.cloned.1.call-start = ((), (), s32[]{:S(2)}) async-start(), calls=%async_computation.1 | async-start | bytes 4456448 | tf_op jit(solution)/shard_map/reduce_scatter | solution.py:61
  17.3 142.0 %all-reduce.13.cloned.1.call-start = ((), (), s32[]{:S(2)}) async-start(), calls=%async_computation.2 | async-start | bytes 524288 | tf_op jit(solution)/shard_map/psum | solution.py:70
  97.5 147.9 %all-reduce.15.cloned.1.call-start = ((), (), s32[]{:S(2)}) async-start(), calls=%async_computation.3 | async-start | bytes 327680 | tf_op jit(solution)/shard_map/psum | solution.py:73
  159.4 159.0 %copy-start.2 = (f32[64,1024]{1,0:T(8,128)S(1)}, f32[64,1024]{1,0:T(8,128)}, u32[]{:S(2)}) copy-start(f32[64,1024]{1,0:T(8,128)} %all-reduce.13.cloned.1.call-done) | copy-start | bytes 786436
  162.2 240.6 %all-reduce.17.cloned.1.call-start = ((), (), s32[]{:S(2)}) async-start(), calls=%async_computation.4 | async-start | bytes 327680 | tf_op jit(solution)/shard_map/psum | solution.py:73
  320.1 240.2 %all-reduce.19.cloned.1.call-start = ((), (), s32[]{:S(2)}) async-start(), calls=%async_computation.5 | async-start | bytes 327680 | tf_op jit(solution)/shard_map/psum | solution.py:73
  477.6 240.2 %all-reduce.21.cloned.1.call-start = ((), (), s32[]{:S(2)}) async-start(), calls=%async_computation.6 | async-start | bytes 327680 | tf_op jit(solution)/shard_map/psum | solution.py:73
  635.0 240.2 %all-reduce.23.cloned.1.call-start = ((), (), s32[]{:S(2)}) async-start(), calls=%async_computation.7 | async-start | bytes 327680 | tf_op jit(solution)/shard_map/psum | solution.py:73
  792.5 158.4 %all-gather.2.cloned.1.call-start = ((), (), s32[]{:S(2)}) async-start(), calls=%async_computation.11 | async-start | bytes 4718592 | tf_op jit(solution)/shard_map/all_gather | solution.py:58
  793.4 239.2 %all-reduce.25.cloned.1.call-start = ((), (), s32[]{:S(2)}) async-start(), calls=%async_computation.8 | async-start | bytes 327680 | tf_op jit(solution)/shard_map/psum | solution.py:73
  793.5 5.9 copy-start.4
  832.0 118.0 %copy-start.3 = (f32[8,128,256]{2,1,0:T(8,128)S(1)}, f32[8,128,256]{2,1,0:T(8,128)}, u32[]{:S(2)}) copy-start(f32[8,128,256]{2,1,0:T(8,128)} %get-tuple-element.51) | copy-start | bytes 3145732
  949.9 240.2 %all-reduce.27.cloned.1.call-start = ((), (), s32[]{:S(2)}) async-start(), calls=%async_computation.9 | async-start | bytes 327680 | tf_op jit(solution)/shard_map/psum | solution.py:73
  1107.4 240.4 %all-reduce.29.cloned.1.call-start = ((), (), s32[]{:S(2)}) async-start(), calls=%async_computation.10 | async-start | bytes 327680 | tf_op jit(solution)/shard_map/psum | solution.py:73
  1397.7 29.0 %copy-start.1 = (f32[160,1024]{1,0:T(8,128)S(1)}, f32[160,1024]{1,0:T(8,128)}, u32[]{:S(2)}) copy-start(f32[160,1024]{1,0:T(8,128)} %param.14) | copy-start | bytes 1966084
Sparse Core Ops, SparseCore 0:
  17.5 79.9 reduce-scatter.1
  99.9 59.4 all-reduce.12
  163.2 82.1 all-reduce.14
  320.2 82.5 all-reduce.16
  477.7 82.5 all-reduce.18
  635.1 82.5 all-reduce.20
  792.6 82.5 all-reduce.22
  877.5 31.3 all-gather.1
  950.1 82.5 all-reduce.24
  1107.5 82.5 all-reduce.26
  1265.3 82.5 all-reduce.28
where the time goes:
time: 1440 us; the launch traced here: 1430 us
  waiting for transfers between devices  715 us (50%)
  other arithmetic  386 us (27%)
  blocking collectives  199 us (14%)
  matrix products  65.8 us (5%)
  local copies, waits for them, and re-layouts  39.1 us (3%)
  between operations  25.9 us (2%)
    psum x8, waiting for transfers between devices, local(): moment = lax.psum(moment_of(product), 'kv')  573 us
    another operation x56, other arithmetic, solve_lower(): jnp.linalg.cholesky(moment)  206 us
    all_gather x8, blocking collectives, local(): subspace = lax.all_gather(basis_piece, 'kv', axis=1, tiled=True)  186 us
    another operation x42, other arithmetic, solve_lower(): jax.scipy.linalg.solve_triangular(jnp.linalg.cholesky(moment), product, l...  158 us
    reduce_scatter x1, waiting for transfers between devices, local(): lax.psum_scatter(lax.dot_general(prefill_keys, prefill_keys, (((0,), (0,)...  80.1 us
    psum x1, waiting for transfers between devices, local(): gram_rows = lax.psum(gram_block, 'seq')  61.8 us
    dot_general x16, matrix products, one_head(): jnp.einsum('qgd,cd->qgc', query_group, key_group, preferred_element_type=...  29.6 us
  transfers between devices with their start and end apart: 11, of which 10 were waited for; matrix products, arithmetic and copies ran while one was open for 9% of the time, Pallas kernels for 0%

commit v1 on v0

--- a/solution.py
+++ b/solution.py
@@ -70,7 +70,7 @@
     gram_rows = lax.psum(gram_block, "seq")
     for iteration in range(ITERS):
         product = apply_gram(subspace, gram_rows)
-        moment = lax.psum(moment_of(product), "kv")
+        moment = jnp.sum(lax.all_gather(moment_of(product), "kv"), axis=0)
         basis_piece = solve_lower(moment, product)
         subspace = lax.all_gather(basis_piece, "kv", axis=1, tiled=True)
     rounded = subspace.astype(jnp.bfloat16)

time: 1440 us -> 1150 us (0.80)
  waiting for transfers between devices: 715 us -> 412 us
    psum x8 -> x0, waiting for transfers between devices: 573 us -> none  [local(): moment = lax.psum(moment_of(product), 'kv')]
    all_gather x0 -> x8, waiting for transfers between devices: none -> 270 us  [local(): moment = jnp.sum(lax.all_gather(moment_of(product), 'kv'), axis=0)]
    reduce_sum x0 -> x8, other arithmetic: none -> 15.4 us  [local(): moment = jnp.sum(lax.all_gather(moment_of(product), 'kv'), axis=0)]
  transfers between devices with their start and end apart: 11 -> 11, of which waited for: 10 -> 9; matrix products, arithmetic and copies ran while one was open for 9% -> 11% of each run, Pallas kernels for 0% -> 0%
where the time goes in v1:
time: 1150 us; the launch traced here: 1140 us
  waiting for transfers between devices  412 us (36%)
  other arithmetic  395 us (34%)
  blocking collectives  209 us (18%)
  matrix products  65.8 us (6%)
  local copies, waits for them, and re-layouts  31.6 us (3%)
  between operations  25.7 us (2%)
    all_gather x8, waiting for transfers between devices, local(): moment = jnp.sum(lax.all_gather(moment_of(product), 'kv'), axis=0)  270 us
    another operation x56, other arithmetic, solve_lower(): jnp.linalg.cholesky(moment)  206 us
    all_gather x8, blocking collectives, local(): subspace = lax.all_gather(basis_piece, 'kv', axis=1, tiled=True)  195 us
    another operation x42, other arithmetic, solve_lower(): jax.scipy.linalg.solve_triangular(jnp.linalg.cholesky(moment), product, l...  158 us
    reduce_scatter x1, waiting for transfers between devices, local(): lax.psum_scatter(lax.dot_general(prefill_keys, prefill_keys, (((0,), (0,)...  80.1 us
    psum x1, waiting for transfers between devices, local(): gram_rows = lax.psum(gram_block, 'seq')  61.9 us
    dot_general x16, matrix products, one_head(): jnp.einsum('qgd,cd->qgc', query_group, key_group, preferred_element_type=...  29.6 us
  transfers between devices with their start and end apart: 11, of which 9 were waited for; matrix products, arithmetic and copies ran while one was open for 11% of the time, Pallas kernels for 0%

profile of v1, /device:TPU:0, one launch (start us, length us, event | category | flops | bytes accessed | tf_op | source)
XLA Modules:
  0.0 1142.0 jit_solution(9140807122874861171)
XLA Ops:
  7.2 10.1 convolution_multiply_fusion
  17.4 80.1 %reduce-scatter.2.cloned.1.call-done = f32[64,1024]{1,0:T(8,128)} async-done(((f32[1024,1024]{1,0:T(8,128)}), f32[64,1024]{1,0:T(8,128)}) %reduce-scatter.2.cloned.1.call-update) | async-done | bytes 262160 | tf_op jit(solution)/shard_map/reduce_scatter | solution.py:61
  97.5 61.9 %all-reduce.5.cloned.1.call-done = f32[64,1024]{1,0:T(8,128)} async-done(((f32[64,1024]{1,0:T(8,128)}), f32[64,1024]{1,0:T(8,128)}) %all-reduce.5.cloned.1.call-update) | async-done | bytes 262160 | tf_op jit(solution)/shard_map/psum | solution.py:70
  162.8 44.7 %all-gather.20.cloned.1.call-done = f32[2560,160]{1,0:T(8,128)} async-done(((f32[160,160]{1,0:T(8,128)}), f32[2560,160]{1,0:T(8,128)}) %all-gather.20.cloned.1.call-update) | async-done | bytes 1638416 | tf_op jit(solution)/shard_map/all_gather | solution.py:73
  209.6 11.7 %cholesky.412 = f32[128,128]{1,0:T(8,128)S(1)} custom-call(f32[128,128]{1,0:T(8,128)S(1)} %cholesky.712), custom_call_target="Cholesky" | custom-call | tf_op jit(solution)/shard_map/jit(cholesky)/cholesky | solution.py:21
  221.4 9.8 custom-call.25
  237.2 19.7 %custom-call.26 = f32[2,128,128]{1,2,0:T(8,128)S(1)} custom-call(f32[2,128,128]{2,1,0:T(8,128)S(1)} %pad_maximum_fusion), custom_call_target="InvertDiagBlocksLowerTriangular" | custom-call | tf_op jit(solution)/shard_map/jit(_solve_triangular)/triangular_solve | solution.py:21
  257.4 24.6 %all_gather.80 = f32[160,1024]{0,1:T(8,128)S(1)} all-gather(f32[160,64]{0,1:T(8,128)S(1)} %pad_maximum_fusion.8), channel_id=1, replica_groups=mesh['kv'=16,'seq'=8] {'kv'}, dimensions={1}, use_global_device_ids=true | all-gather | bytes 696320 | tf_op jit(solution)/shard_map/all_gather | solution.py:75
  284.0 44.4 %all-gather.22.cloned.1.call-done = f32[2560,160]{1,0:T(8,128)} async-done(((f32[160,160]{1,0:T(8,128)}), f32[2560,160]{1,0:T(8,128)}) %all-gather.22.cloned.1.call-update) | async-done | bytes 1638416 | tf_op jit(solution)/shard_map/all_gather | solution.py:73
  330.5 11.7 %cholesky.450 = f32[128,128]{1,0:T(8,128)S(1)} custom-call(f32[128,128]{1,0:T(8,128)S(1)} %cholesky.715), custom_call_target="Cholesky" | custom-call | tf_op jit(solution)/shard_map/jit(cholesky)/cholesky | solution.py:21
  342.3 9.8 custom-call.27
  358.1 19.7 %custom-call.28 = f32[2,128,128]{1,2,0:T(8,128)S(1)} custom-call(f32[2,128,128]{2,1,0:T(8,128)S(1)} %pad_maximum_fusion.1), custom_call_target="InvertDiagBlocksLowerTriangular" | custom-call | tf_op jit(solution)/shard_map/jit(_solve_triangular)/triangular_solve | solution.py:21
  378.3 24.6 %all_gather.83 = f32[160,1024]{0,1:T(8,128)S(1)} all-gather(f32[160,64]{0,1:T(8,128)S(1)} %pad_maximum_fusion.9), channel_id=1, replica_groups=mesh['kv'=16,'seq'=8] {'kv'}, dimensions={1}, use_global_device_ids=true | all-gather | bytes 696320 | tf_op jit(solution)/shard_map/all_gather | solution.py:75
  405.0 44.4 %all-gather.24.cloned.1.call-done = f32[2560,160]{1,0:T(8,128)} async-done(((f32[160,160]{1,0:T(8,128)}), f32[2560,160]{1,0:T(8,128)}) %all-gather.24.cloned.1.call-update) | async-done | bytes 1638416 | tf_op jit(solution)/shard_map/all_gather | solution.py:73
  451.4 11.7 %cholesky.488 = f32[128,128]{1,0:T(8,128)S(1)} custom-call(f32[128,128]{1,0:T(8,128)S(1)} %cholesky.718), custom_call_target="Cholesky" | custom-call | tf_op jit(solution)/shard_map/jit(cholesky)/cholesky | solution.py:21
  463.2 9.8 custom-call.29
  479.0 19.7 %custom-call.30 = f32[2,128,128]{1,2,0:T(8,128)S(1)} custom-call(f32[2,128,128]{2,1,0:T(8,128)S(1)} %pad_maximum_fusion.2), custom_call_target="InvertDiagBlocksLowerTriangular" | custom-call | tf_op jit(solution)/shard_map/jit(_solve_triangular)/triangular_solve | solution.py:21
  499.3 24.6 %all_gather.86 = f32[160,1024]{0,1:T(8,128)S(1)} all-gather(f32[160,64]{0,1:T(8,128)S(1)} %pad_maximum_fusion.10), channel_id=1, replica_groups=mesh['kv'=16,'seq'=8] {'kv'}, dimensions={1}, use_global_device_ids=true | all-gather | bytes 696320 | tf_op jit(solution)/shard_map/all_gather | solution.py:75
  526.1 44.4 %all-gather.26.cloned.1.call-done = f32[2560,160]{1,0:T(8,128)} async-done(((f32[160,160]{1,0:T(8,128)}), f32[2560,160]{1,0:T(8,128)}) %all-gather.26.cloned.1.call-update) | async-done | bytes 1638416 | tf_op jit(solution)/shard_map/all_gather | solution.py:73
  572.5 11.7 %cholesky.526 = f32[128,128]{1,0:T(8,128)S(1)} custom-call(f32[128,128]{1,0:T(8,128)S(1)} %cholesky.721), custom_call_target="Cholesky" | custom-call | tf_op jit(solution)/shard_map/jit(cholesky)/cholesky | solution.py:21
  584.3 9.8 custom-call.31
  600.1 19.7 %custom-call.32 = f32[2,128,128]{1,2,0:T(8,128)S(1)} custom-call(f32[2,128,128]{2,1,0:T(8,128)S(1)} %pad_maximum_fusion.3), custom_call_target="InvertDiagBlocksLowerTriangular" | custom-call | tf_op jit(solution)/shard_map/jit(_solve_triangular)/triangular_solve | solution.py:21
  620.4 24.6 %all_gather.89 = f32[160,1024]{0,1:T(8,128)S(1)} all-gather(f32[160,64]{0,1:T(8,128)S(1)} %pad_maximum_fusion.11), channel_id=1, replica_groups=mesh['kv'=16,'seq'=8] {'kv'}, dimensions={1}, use_global_device_ids=true | all-gather | bytes 696320 | tf_op jit(solution)/shard_map/all_gather | solution.py:75
  647.0 44.6 %all-gather.28.cloned.1.call-done = f32[2560,160]{1,0:T(8,128)} async-done(((f32[160,160]{1,0:T(8,128)}), f32[2560,160]{1,0:T(8,128)}) %all-gather.28.cloned.1.call-update) | async-done | bytes 1638416 | tf_op jit(solution)/shard_map/all_gather | solution.py:73
  693.6 11.7 %cholesky.564 = f32[128,128]{1,0:T(8,128)S(1)} custom-call(f32[128,128]{1,0:T(8,128)S(1)} %cholesky.724), custom_call_target="Cholesky" | custom-call | tf_op jit(solution)/shard_map/jit(cholesky)/cholesky | solution.py:21
  705.4 9.8 custom-call.33
  721.3 19.7 %custom-call.34 = f32[2,128,128]{1,2,0:T(8,128)S(1)} custom-call(f32[2,128,128]{2,1,0:T(8,128)S(1)} %pad_maximum_fusion.4), custom_call_target="InvertDiagBlocksLowerTriangular" | custom-call | tf_op jit(solution)/shard_map/jit(_solve_triangular)/triangular_solve | solution.py:21
  741.5 24.6 %all_gather.92 = f32[160,1024]{0,1:T(8,128)S(1)} all-gather(f32[160,64]{0,1:T(8,128)S(1)} %pad_maximum_fusion.12), channel_id=1, replica_groups=mesh['kv'=16,'seq'=8] {'kv'}, dimensions={1}, use_global_device_ids=true | all-gather | bytes 696320 | tf_op jit(solution)/shard_map/all_gather | solution.py:75
  767.9 5.5 convert_reduce_fusion
  774.7 38.0 %all-gather.30.cloned.1.call-done = f32[2560,160]{1,0:T(8,128)} async-done(((f32[160,160]{1,0:T(8,128)}), f32[2560,160]{1,0:T(8,128)}) %all-gather.30.cloned.1.call-update) | async-done | bytes 1638416 | tf_op jit(solution)/shard_map/all_gather | solution.py:73
  814.8 11.7 %cholesky.602 = f32[128,128]{1,0:T(8,128)S(1)} custom-call(f32[128,128]{1,0:T(8,128)S(1)} %cholesky.727), custom_call_target="Cholesky" | custom-call | tf_op jit(solution)/shard_map/jit(cholesky)/cholesky | solution.py:21
  826.5 9.8 custom-call.35
  842.4 19.7 %custom-call.36 = f32[2,128,128]{1,2,0:T(8,128)S(1)} custom-call(f32[2,128,128]{2,1,0:T(8,128)S(1)} %pad_maximum_fusion.5), custom_call_target="InvertDiagBlocksLowerTriangular" | custom-call | tf_op jit(solution)/shard_map/jit(_solve_triangular)/triangular_solve | solution.py:21
  862.6 24.4 %all_gather.95 = f32[160,1024]{0,1:T(8,128)S(1)} all-gather(f32[160,64]{0,1:T(8,128)S(1)} %pad_maximum_fusion.13), channel_id=1, replica_groups=mesh['kv'=16,'seq'=8] {'kv'}, dimensions={1}, use_global_device_ids=true | all-gather | bytes 696320 | tf_op jit(solution)/shard_map/all_gather | solution.py:75
  897.7 13.8 %all_gather.103 = bf16[256,1024]{1,0:T(8,128)(2,1)S(1)} all-gather(bf16[32,1024]{1,0:T(8,128)(2,1)S(1)} %bitcast_select_fusion), channel_id=1, replica_groups=mesh['kv'=16,'seq'=8] {'seq'}, dimensions={0}, use_global_device_ids=true | all-gather | bytes 589824 | tf_op jit(solution)/shard_map/all_gather | solution.py:59
  911.7 15.4 %while.30 = (s32[]{:T(128)}, f32[8,128,256]{2,1,0:T(8,128)}, bf16[8,128,8,128]{3,1,2,0:T(8,128)(2,1)}, bf16[8,256,128]{1,2,0:T(8,128)(2,1)S(1)}, s32[]{:T(128)}) while((s32[]{:T(128)}, f32[8,128,256]{2,1,0:T(8,128)}, bf16[8,128,8,128]{3,1,2,0:T(8,128)(2,1)}, bf16[8,256,128]{1,2,0:T(8,128)(2,1)S(1)}, s32[]{:T(128)}) %tuple.133), condition=%wide.region_20.23_spmd, body=%wide.region_18.22_spmd.sunk | while | flops 67338240 | bytes 722493 | solution.py:56
  929.2 6.4 copy.89
  937.7 11.7 %cholesky.640 = f32[128,128]{1,0:T(8,128)S(1)} custom-call(f32[128,128]{1,0:T(8,128)S(1)} %cholesky.730), custom_call_target="Cholesky" | custom-call | tf_op jit(solution)/shard_map/jit(cholesky)/cholesky | solution.py:21
  949.5 9.8 custom-call.37
  965.3 19.7 %custom-call.38 = f32[2,128,128]{1,2,0:T(8,128)S(1)} custom-call(f32[2,128,128]{2,1,0:T(8,128)S(1)} %pad_maximum_fusion.6), custom_call_target="InvertDiagBlocksLowerTriangular" | custom-call | tf_op jit(solution)/shard_map/jit(_solve_triangular)/triangular_solve | solution.py:21
  985.6 22.7 %all_gather.98 = f32[160,1024]{0,1:T(8,128)S(1)} all-gather(f32[160,64]{0,1:T(8,128)S(1)} %pad_maximum_fusion.14), channel_id=1, replica_groups=mesh['kv'=16,'seq'=8] {'kv'}, dimensions={1}, use_global_device_ids=true | all-gather | bytes 696320 | tf_op jit(solution)/shard_map/all_gather | solution.py:75
  1010.1 28.5 %while.29 = (s32[]{:T(128)}, f32[8,128,2048]{2,1,0:T(8,128)}, bf16[8,128,8,128]{3,1,2,0:T(8,128)(2,1)}, bf16[8,2048,128]{1,2,0:T(8,128)(2,1)}, s32[]{:T(128)}) while((s32[]{:T(128)}, f32[8,128,2048]{2,1,0:T(8,128)}, bf16[8,128,8,128]{3,1,2,0:T(8,128)(2,1)}, bf16[8,2048,128]{1,2,0:T(8,128)(2,1)}, s32[]{:T(128)}) %tuple.132), condition=%wide.region_17.20_spmd, body=%wide.region_15.19_spmd.sunk | while | flops 538705920 | bytes 3933757 | solution.py:56
  1038.6 6.6 multiply_convert_fusion
  1045.2 9.7 all-gather.34.cloned.1.call-done
  1057.0 11.7 %cholesky.678 = f32[128,128]{1,0:T(8,128)S(1)} custom-call(f32[128,128]{1,0:T(8,128)S(1)} %cholesky.733), custom_call_target="Cholesky" | custom-call | tf_op jit(solution)/shard_map/jit(cholesky)/cholesky | solution.py:21
  1068.8 9.8 custom-call.39
  1084.6 19.7 %custom-call.40 = f32[2,128,128]{1,2,0:T(8,128)S(1)} custom-call(f32[2,128,128]{2,1,0:T(8,128)S(1)} %pad_maximum_fusion.7), custom_call_target="InvertDiagBlocksLowerTriangular" | custom-call | tf_op jit(solution)/shard_map/jit(_solve_triangular)/triangular_solve | solution.py:21
  1104.8 24.7 %all_gather.101 = f32[160,1024]{0,1:T(8,128)S(1)} all-gather(f32[160,64]{0,1:T(8,128)S(1)} %pad_maximum_fusion.15), channel_id=1, replica_groups=mesh['kv'=16,'seq'=8] {'kv'}, dimensions={1}, use_global_device_ids=true | all-gather | bytes 696320 | tf_op jit(solution)/shard_map/all_gather | solution.py:75
  (265 shorter events, 137.2 us)
Async XLA Ops:
  7.2 152.2 %copy-start = (f32[160,1024]{1,0:T(8,128)S(1)}, f32[160,1024]{1,0:T(8,128)}, u32[]{:S(2)}) copy-start(f32[160,1024]{1,0:T(8,128)} %param.14) | copy-start | bytes 1966084
  7.2 90.3 %reduce-scatter.2.cloned.1.call-start = ((), (), s32[]{:S(2)}) async-start(), calls=%async_computation.1 | async-start | bytes 4456448 | tf_op jit(solution)/shard_map/reduce_scatter | solution.py:61
  17.3 142.0 %all-reduce.5.cloned.1.call-start = ((), (), s32[]{:S(2)}) async-start(), calls=%async_computation.2 | async-start | bytes 524288 | tf_op jit(solution)/shard_map/psum | solution.py:70
  97.5 110.1 %all-gather.20.cloned.1.call-start = ((), (), s32[]{:S(2)}) async-start(), calls=%async_computation.4 | async-start | bytes 2785280 | tf_op jit(solution)/shard_map/all_gather | solution.py:73
  159.4 122.6 %copy-start.2 = (f32[64,1024]{1,0:T(8,128)S(1)}, f32[64,1024]{1,0:T(8,128)}, u32[]{:S(2)}) copy-start(f32[64,1024]{1,0:T(8,128)} %all-reduce.5.cloned.1.call-done) | copy-start | bytes 786436
  162.2 166.2 %all-gather.22.cloned.1.call-start = ((), (), s32[]{:S(2)}) async-start(), calls=%async_computation.5 | async-start | bytes 2785280 | tf_op jit(solution)/shard_map/all_gather | solution.py:73
  283.8 165.5 %all-gather.24.cloned.1.call-start = ((), (), s32[]{:S(2)}) async-start(), calls=%async_computation.6 | async-start | bytes 2785280 | tf_op jit(solution)/shard_map/all_gather | solution.py:73
  404.7 165.7 %all-gather.26.cloned.1.call-start = ((), (), s32[]{:S(2)}) async-start(), calls=%async_computation.7 | async-start | bytes 2785280 | tf_op jit(solution)/shard_map/all_gather | solution.py:73
  525.6 165.9 %all-gather.28.cloned.1.call-start = ((), (), s32[]{:S(2)}) async-start(), calls=%async_computation.8 | async-start | bytes 2785280 | tf_op jit(solution)/shard_map/all_gather | solution.py:73
  646.7 165.9 %all-gather.30.cloned.1.call-start = ((), (), s32[]{:S(2)}) async-start(), calls=%async_computation.9 | async-start | bytes 2785280 | tf_op jit(solution)/shard_map/all_gather | solution.py:73
  767.8 161.4 %all-gather.18.cloned.1.call-start = ((), (), s32[]{:S(2)}) async-start(), calls=%async_computation.3 | async-start | bytes 4718592 | tf_op jit(solution)/shard_map/all_gather | solution.py:58
  774.3 161.4 %all-gather.32.cloned.1.call-start = ((), (), s32[]{:S(2)}) async-start(), calls=%async_computation.10 | async-start | bytes 2785280 | tf_op jit(solution)/shard_map/all_gather | solution.py:73
  812.7 76.1 %copy-start.3 = (s32[4]{0:T(128)S(1)}, s32[4]{0:T(128)}, u32[]{:S(2)}) copy-start(s32[4]{0:T(128)} %param.13) | copy-start | bytes 52
  888.7 166.2 %all-gather.34.cloned.1.call-start = ((), (), s32[]{:S(2)}) async-start(), calls=%async_computation.11 | async-start | bytes 2785280 | tf_op jit(solution)/shard_map/all_gather | solution.py:73
  1104.8 30.4 %copy-start.1 = (f32[160,1024]{1,0:T(8,128)S(1)}, f32[160,1024]{1,0:T(8,128)}, u32[]{:S(2)}) copy-start(f32[160,1024]{1,0:T(8,128)} %param.14) | copy-start | bytes 1966084
Sparse Core Ops, SparseCore 0:
  17.5 79.9 reduce-scatter.1
  99.9 59.4 all-reduce.4
  162.4 45.1 all-gather.19
  283.9 44.4 all-gather.21
  404.8 44.4 all-gather.23
  525.7 44.6 all-gather.25
  646.8 44.6 all-gather.27
  768.0 44.6 all-gather.29
  815.0 31.8 all-gather.17
  888.9 44.7 all-gather.31
  1010.2 44.6 all-gather.33
